TPU v7x, 256 devices: a whole 4x4x8 slice. The times are simulated.
256 devices in a mesh: seq: 64 (over z, x, core), head: 4 (over y).
Axes of the slice: x: 4, y: 4, z: 8, core: 2. Of those that a mesh axis runs over, the one named last changes fastest.
Arguments:
- features: bfloat16 [8192, 4096], P('seq', 'head'), may hold values from -6 to 6
- proj_weight: bfloat16 [4096, 4096], P(None, 'head'), may hold values from -0.09375 to 0.09375
- query_vectors: bfloat16 [8192, 4096], P('seq', 'head'), may hold values from -6 to 6
- key_vectors: bfloat16 [8192, 4096], P('seq', 'head'), may hold values from -6 to 6
Outputs:
- rotated_queries: bfloat16 [8192, 4096], P('seq', 'head')
- rotated_keys: bfloat16 [8192, 4096], P('seq', 'head')
All inputs are finite; a program needn't handle non-finite values.
Results may differ from a plain program's by a relative error of at most 0.0024.
Values may be sent and summed in bfloat16 or wider, within the bound.
No kernel may reach another device: no remote copies, remote signals or barrier semaphores. Data moves between devices by JAX's collectives and lax.ppermute only.
A program may use at most 128 MiB of HBM per device.

v0:
```python
import jax
import jax.numpy as jnp
from jax import lax
from jax.sharding import PartitionSpec as P

HEAD_DIM = 128


def entering(array, axis, combine, identity):
    count, place = (lax.axis_size(axis), lax.axis_index(axis))
    everything = lax.all_gather(array, axis)
    start = jnp.broadcast_to(jnp.asarray(identity, array.dtype), array.shape)

    def turn(k, before):
        reached = k < place
        new = combine(before, everything[k])
        return jnp.where(reached, new, before)

    return lax.fori_loop(0, count, turn, start)


def small_inverse(matrix):
    highest = lax.Precision.HIGHEST
    size = matrix.shape[-1]
    position = jnp.arange(size)
    strict = (position[:, None] < position[None, :]).astype(jnp.float32)
    eye_block = jnp.eye(size, dtype=jnp.float32)
    power = -2.0 * matrix * strict[None]
    result = eye_block[None] + power
    reach = 2
    while reach < size:
        power = jnp.einsum("hij,hjk->hik", power, power, precision=highest)
        result = result + jnp.einsum("hij,hjk->hik", result, power, precision=highest)
        reach = reach * 2
    return 2.0 * result


def triangle_inverse(matrix):
    highest = lax.Precision.HIGHEST
    size = matrix.shape[-1]
    if size <= 16:
        return small_inverse(matrix)
    half = size // 2
    first = triangle_inverse(matrix[:, :half, :half])
    second = triangle_inverse(matrix[:, half:, half:])
    coupling = matrix[:, :half, half:]
    middle = jnp.einsum("hij,hjk->hik", first, coupling, precision=highest)
    corner = -jnp.einsum("hij,hjk->hik", middle, second, precision=highest)
    lower_left = jnp.zeros((matrix.shape[0], size - half, half), jnp.float32)
    top = jnp.concatenate([first, corner], axis=2)
    bottom = jnp.concatenate([lower_left, second], axis=2)
    return jnp.concatenate([top, bottom], axis=1)


def upper_solve(matrix, right_side):
    highest = lax.Precision.HIGHEST
    rows = matrix.shape[1]
    size = min(128, rows)
    count = rows // size
    solved_blocks = []
    for i in reversed(range(count)):
        inverse_block = triangle_inverse(matrix)
        solved_blocks.append(
            jnp.einsum("hij,hjk->hik", inverse_block, right_side, precision=highest)
        )
    return jnp.concatenate(solved_blocks[::-1], axis=1)


def body(features, proj_weight, query_vectors, key_vectors):
    highest = lax.Precision.HIGHEST
    tok_rows = query_vectors.shape[0]
    width = proj_weight.shape[1]
    local_heads = width // HEAD_DIM
    raw_proj = jnp.dot(
        lax.all_gather(features, "head", axis=1, tiled=True),
        proj_weight,
        preferred_element_type=jnp.float32,
    )
    raw_proj = raw_proj.reshape(tok_rows, local_heads, HEAD_DIM)
    directions = raw_proj * lax.rsqrt(jnp.sum(raw_proj * raw_proj, axis=-1, keepdims=True) + 1e-06)
    reflectors = jnp.transpose(directions, (1, 0, 2))
    targets = jnp.concatenate(
        [
            query_vectors.reshape(tok_rows, local_heads, HEAD_DIM),
            key_vectors.reshape(tok_rows, local_heads, HEAD_DIM),
        ],
        axis=0,
    )
    targets = jnp.transpose(targets.astype(jnp.float32), (1, 0, 2))
    gram = jnp.einsum("hid,hjd->hij", reflectors, reflectors, precision=highest)
    position = jnp.arange(tok_rows)
    upper = (position[:, None] < position[None, :]).astype(jnp.float32)
    identity_tok = jnp.eye(tok_rows, dtype=jnp.float32)
    inverse_t = gram * upper[None] + 0.5 * identity_tok[None]
    projected = jnp.einsum("hid,htd->hit", reflectors, targets, precision=highest)
    target_pos = jnp.concatenate([position, position])
    keep = (position[:, None] <= target_pos[None, :]).astype(jnp.float32)
    masked = projected * keep[None]
    right_side = jnp.concatenate([masked, reflectors], axis=2)
    solved = upper_solve(inverse_t, right_side)
    weights_tok = solved[:, :, : 2 * tok_rows]
    factor = solved[:, :, 2 * tok_rows :]
    local_part = targets - jnp.einsum("hit,hid->htd", weights_tok, reflectors, precision=highest)
    identity = jnp.broadcast_to(
        jnp.eye(HEAD_DIM, dtype=jnp.float32), (local_heads, HEAD_DIM, HEAD_DIM)
    )
    block_product = identity - jnp.einsum("hid,hie->hde", reflectors, factor, precision=highest)

    def combine(earlier, later):
        return jnp.einsum("hde,hef->hdf", earlier, later, precision=highest)

    carried = entering(block_product, "seq", combine, identity)
    rotated = jnp.einsum("hde,hte->htd", carried, local_part, precision=highest)
    rotated = jnp.transpose(rotated, (1, 0, 2))
    rotated_queries = rotated[:tok_rows].reshape(tok_rows, width).astype(jnp.bfloat16)
    rotated_keys = rotated[tok_rows:].reshape(tok_rows, width).astype(jnp.bfloat16)
    return (rotated_queries, rotated_keys)


def solution(mesh):
    in_specs = (P("seq", "head"), P(None, "head"), P("seq", "head"), P("seq", "head"))
    out_specs = (P("seq", "head"), P("seq", "head"))
    return jax.shard_map(body, mesh=mesh, in_specs=in_specs, out_specs=out_specs, check_vma=False)
```

profile of v0, /device:TPU:1, one launch (start us, length us, event | category | flops | bytes accessed | tf_op | source)
XLA Modules:
  0.0 355.1 jit_solution(6094807427301237134)
XLA Ops:
  10.7 27.5 %all-gather.4.cloned.1.call-done = bf16[128,4096]{1,0:T(8,128)(2,1)} async-done(((bf16[128,1024]{1,0:T(8,128)(2,1)}), bf16[128,4096]{1,0:T(8,128)(2,1)}) %all-gather.4.cloned.1.call-update) | async-done | bytes 1048592 | tf_op jit(solution)/shard_map/all_gather | solution.py:75
  38.2 5.0 %fusion.124 = f32[128,1024]{1,0:T(8,128)S(1)} fusion(bf16[128,4096]{1,0:T(8,128)(2,1)} %all-gather.4.cloned.1.call-done, bf16[4096,1024]{1,0:T(8,128)(2,1)} %param.7), kind=kOutput, calls=%fused_computation.185 | convolution fusion | flops 1073741824 | bytes 9961472 | tf_op jit(solution)/shard_map/dot_general | solution.py:74
  64.4 2.9 convolution_subtract_fusion
  67.3 141.6 %all-gather.6.cloned.1.call-done = f32[512,128,128]{2,1,0:T(8,128)} async-done(((f32[8,128,128]{2,1,0:T(8,128)}), f32[512,128,128]{2,1,0:T(8,128)}) %all-gather.6.cloned.1.call-update) | async-done | bytes 33554448 | tf_op jit(solution)/shard_map/all_gather | solution.py:11
  208.9 136.5 %while.13 = (s32[]{:T(128)}, f32[8,128,128]{1,2,0:T(8,128)S(1)}, s32[]{:T(128)}, f32[64,8,128,128]{3,2,1,0:T(8,128)}, s32[]{:T(128)}) while((s32[]{:T(128)}, f32[8,128,128]{1,2,0:T(8,128)S(1)}, s32[]{:T(128)}, f32[64,8,128,128]{3,2,1,0:T(8,128)}, s32[]{:T(128)}) %tuple.48), condition=%wide.region_2.3_spmd, body=%wide.region_1.2_spmd.sunk | while | flops 201457664 | bytes 3145811 | solution.py:19
  208.9 2.1 fusion.247
  219.6 2.1 fusion.247
  230.3 2.1 fusion.247
  238.8 2.1 fusion.247
  240.9 2.1 fusion.247
  249.5 2.1 fusion.247
  260.1 2.1 fusion.247
  268.7 2.1 fusion.247
  279.3 2.1 fusion.247
  285.7 2.1 fusion.247
  287.8 2.1 fusion.247
  298.5 2.1 fusion.247
  304.9 2.1 fusion.247
  307.0 2.1 fusion.247
  317.7 2.1 fusion.247
  324.1 2.1 fusion.247
  326.2 2.1 fusion.247
  336.9 2.1 fusion.247
  343.3 2.1 fusion.247
  (210 shorter events, 122.1 us)
Async XLA Ops:
  7.2 31.0 %all-gather.4.cloned.1.call-start = ((), (), s32[]{:S(2)}) async-start(), calls=%async_computation | async-start | bytes 1310720 | tf_op jit(solution)/shard_map/all_gather | solution.py:75
  7.9 201.0 %all-gather.6.cloned.1.call-start = ((), (), s32[]{:S(2)}) async-start(), calls=%async_computation.1 | async-start | bytes 34078720 | tf_op jit(solution)/shard_map/all_gather | solution.py:11
  10.6 49.5 %copy-start = (bf16[128,8,128]{2,0,1:T(8,128)(2,1)}, bf16[128,8,128]{2,0,1:T(8,128)(2,1)S(1)}, u32[]{:S(2)}) copy-start(bf16[128,8,128]{2,0,1:T(8,128)(2,1)S(1)} %copy.41) | copy-start | bytes 786436
Sparse Core Ops, SparseCore 0:
  9.8 28.3 all-gather.3
  64.4 144.4 all-gather.5
where the time goes:
time: 358 us; the launch traced here: 355 us
  waiting for transfers between devices  170 us (47%)
  matrix products  160 us (45%)
  between operations  14.7 us (4%)
  local copies, waits for them, and re-layouts  7.25 us (2%)
    all_gather x1, waiting for transfers between devices, entering(): everything = lax.all_gather(array, axis)  142 us
    dot_general x64, matrix products, combine(): return jnp.einsum('hde,hef->hdf', earlier, later, precision=highest)  132 us
    all_gather x1, waiting for transfers between devices, body(): lax.all_gather(features, 'head', axis=1, tiled=True)  27.5 us
  transfers between devices with their start and end apart: 2, of which 2 were waited for; matrix products, arithmetic and copies ran while one was open for 2% of the time, Pallas kernels for 0%

commit v1 on v0

--- a/solution.py
+++ b/solution.py
@@ -4,6 +4,27 @@
 from jax.sharding import PartitionSpec as P
 
 HEAD_DIM = 128
+
+
+def ring_gather(x, axis, dim):
+    size, position, rows = (lax.axis_size(axis), lax.axis_index(axis), x.shape[dim])
+    ahead = [(i, (i + 1) % size) for i in range(size)]
+    left = [(i, (i - 1) % size) for i in range(size)]
+    filled = jnp.zeros((*x.shape[:dim], size * rows, *x.shape[dim + 1 :]), x.dtype)
+    filled = lax.dynamic_update_slice_in_dim(filled, x, position * rows, axis=dim)
+    from_left = from_right = x
+    half = size // 2
+    for step in range(1, half + 1):
+        from_left = lax.ppermute(from_left, axis, ahead)
+        filled = lax.dynamic_update_slice_in_dim(
+            filled, from_left, (position - step) % size * rows, axis=dim
+        )
+        if step < size - half:
+            from_right = lax.ppermute(from_right, axis, left)
+            filled = lax.dynamic_update_slice_in_dim(
+                filled, from_right, (position + step) % size * rows, axis=dim
+            )
+    return filled
 
 
 def entering(array, axis, combine, identity):
@@ -72,9 +93,7 @@
     width = proj_weight.shape[1]
     local_heads = width // HEAD_DIM
     raw_proj = jnp.dot(
-        lax.all_gather(features, "head", axis=1, tiled=True),
-        proj_weight,
-        preferred_element_type=jnp.float32,
+        ring_gather(features, "head", 1), proj_weight, preferred_element_type=jnp.float32
     )
     raw_proj = raw_proj.reshape(tok_rows, local_heads, HEAD_DIM)
     directions = raw_proj * lax.rsqrt(jnp.sum(raw_proj * raw_proj, axis=-1, keepdims=True) + 1e-06)

time: 358 us -> 346 us (0.966)
  waiting for transfers between devices: 170 us -> 156 us
  starting transfers between devices: 0.08 us -> 3.67 us
    all_gather x1 -> x0, waiting for transfers between devices: 27.5 us -> none  [body(): lax.all_gather(features, 'head', axis=1, tiled=True)]
    ppermute x0 -> x3, waiting for transfers between devices: none -> 14.4 us  [the longest x2 14.4 us: ring_gather(): from_left = lax.ppermute(from_left, axis, ahead)]
    ppermute x0 -> x3, starting transfers between devices: none -> 3.64 us  [the longest x1 3.63 us: ring_gather(): from_right = lax.ppermute(from_right, axis, left)]
  transfers between devices with their start and end apart: 2 -> 4, of which waited for: 2 -> 3; matrix products, arithmetic and copies ran while one was open for 2% -> 1% of each run, Pallas kernels for 0% -> 0%
where the time goes in v1:
time: 346 us; the launch traced here: 343 us
  matrix products  160 us (46%)
  waiting for transfers between devices  156 us (45%)
  between operations  14.8 us (4%)
  local copies, waits for them, and re-layouts  5.56 us (2%)
  starting transfers between devices  3.67 us (1%)
    all_gather x1, waiting for transfers between devices, entering(): everything = lax.all_gather(array, axis)  141 us
    dot_general x64, matrix products, combine(): return jnp.einsum('hde,hef->hdf', earlier, later, precision=highest)  132 us
    ppermute x2, waiting for transfers between devices, ring_gather(): from_left = lax.ppermute(from_left, axis, ahead)  14.4 us
  transfers between devices with their start and end apart: 4, of which 3 were waited for; matrix products, arithmetic and copies ran while one was open for 1% of the time, Pallas kernels for 0%

profile of v1, /device:TPU:1, one launch (start us, length us, event | category | flops | bytes accessed | tf_op | source)
XLA Modules:
  0.0 343.2 jit_solution(2283358836869334327)
XLA Ops:
  7.2 3.6 %collective-permute-start.1 = (bf16[128,1024]{1,0:T(8,128)(2,1)}, bf16[128,1024]{1,0:T(8,128)(2,1)S(1)}, u32[]{:S(2)}, u32[]{:S(2)}) collective-permute-start(bf16[128,1024]{1,0:T(8,128)(2,1)} %param.6), channel_id=1, source_target_pairs={{0,3},{1,0},{2,1},{3,2},{4,7},{5,4},{6,5},{7,6},{8,11},{9,8},{10,9... | collective-permute-start | bytes 786440 | tf_op jit(solution)/shard_map/ppermute | solution.py:23
  11.1 8.1 %collective-permute-done = bf16[128,1024]{1,0:T(8,128)(2,1)S(1)} collective-permute-done((bf16[128,1024]{1,0:T(8,128)(2,1)}, bf16[128,1024]{1,0:T(8,128)(2,1)S(1)}, u32[]{:S(2)}, u32[]{:S(2)}) %collective-permute-start) | collective-permute-done | bytes 262176 | tf_op jit(solution)/shard_map/ppermute | solution.py:18
  20.1 6.3 %collective-permute-done.2 = bf16[128,1024]{1,0:T(8,128)(2,1)S(1)} collective-permute-done((bf16[128,1024]{1,0:T(8,128)(2,1)S(1)}, bf16[128,1024]{1,0:T(8,128)(2,1)S(1)}, u32[]{:S(2)}, u32[]{:S(2)}) %collective-permute-start.2) | collective-permute-done | bytes 262176 | tf_op jit(solution)/shard_map/ppermute | solution.py:18
  26.5 4.7 %fusion.124 = f32[128,1024]{1,0:T(8,128)S(1)} fusion(bf16[128,4096]{1,0:T(8,128)(2,1)S(1)} %constant_dynamic-update-slice_fusion, bf16[4096,1024]{1,0:T(8,128)(2,1)} %param.7), kind=kOutput, calls=%fused_computation.189 | convolution fusion | flops 1073741824 | bytes 9961472 | tf_op jit(solution)/shard_map/dot_general | solution.py:95
  52.5 2.9 convolution_subtract_fusion
  55.4 141.5 %all-gather.3.cloned.1.call-done = f32[512,128,128]{2,1,0:T(8,128)} async-done(((f32[8,128,128]{2,1,0:T(8,128)}), f32[512,128,128]{2,1,0:T(8,128)}) %all-gather.3.cloned.1.call-update) | async-done | bytes 33554448 | tf_op jit(solution)/shard_map/all_gather | solution.py:32
  197.0 136.5 %while.13 = (s32[]{:T(128)}, f32[8,128,128]{1,2,0:T(8,128)S(1)}, s32[]{:T(128)}, f32[64,8,128,128]{3,2,1,0:T(8,128)}, s32[]{:T(128)}) while((s32[]{:T(128)}, f32[8,128,128]{1,2,0:T(8,128)S(1)}, s32[]{:T(128)}, f32[64,8,128,128]{3,2,1,0:T(8,128)}, s32[]{:T(128)}) %tuple.46), condition=%wide.region_2.3_spmd, body=%wide.region_1.2_spmd.sunk | while | flops 201457664 | bytes 3145811 | solution.py:40
  205.5 2.1 fusion.247
  211.9 2.1 fusion.247
  214.1 2.1 fusion.247
  224.7 2.1 fusion.247
  231.1 2.1 fusion.247
  233.3 2.1 fusion.247
  235.4 2.1 fusion.247
  243.9 2.1 fusion.247
  250.3 2.1 fusion.247
  254.6 2.1 fusion.247
  263.1 2.1 fusion.247
  269.5 2.1 fusion.247
  273.8 2.1 fusion.247
  280.2 2.1 fusion.247
  282.3 2.1 fusion.247
  288.7 2.1 fusion.247
  293.0 2.1 fusion.247
  (224 shorter events, 123.9 us)
Async XLA Ops:
  7.2 3.9 %copy-start.1 = (bf16[128,1024]{1,0:T(8,128)(2,1)S(1)}, bf16[128,1024]{1,0:T(8,128)(2,1)}, u32[]{:S(2)}) copy-start(bf16[128,1024]{1,0:T(8,128)(2,1)} %param.6) | copy-start | bytes 786436
  7.2 12.1 %copy-start.2 = (bf16[128,1024]{1,0:T(8,128)(2,1)S(1)}, bf16[128,1024]{1,0:T(8,128)(2,1)}, u32[]{:S(2)}) copy-start(bf16[128,1024]{1,0:T(8,128)(2,1)} %param.8) | copy-start | bytes 786436
  7.2 12.5 %copy-start.3 = (bf16[128,1024]{1,0:T(8,128)(2,1)S(1)}, bf16[128,1024]{1,0:T(8,128)(2,1)}, u32[]{:S(2)}) copy-start(bf16[128,1024]{1,0:T(8,128)(2,1)} %param.9) | copy-start | bytes 786436
  7.2 189.7 %all-gather.3.cloned.1.call-start = ((), (), s32[]{:S(2)}) async-start(), calls=%async_computation | async-start | bytes 34078720 | tf_op jit(solution)/shard_map/all_gather | solution.py:32
  7.2 12.8 %collective-permute-start.1 = (bf16[128,1024]{1,0:T(8,128)(2,1)}, bf16[128,1024]{1,0:T(8,128)(2,1)S(1)}, u32[]{:S(2)}, u32[]{:S(2)}) collective-permute-start(bf16[128,1024]{1,0:T(8,128)(2,1)} %param.6), channel_id=1, source_target_pairs={{0,3},{1,0},{2,1},{3,2},{4,7},{5,4},{6,5},{7,6},{8,11},{9,8},{10,9... | collective-permute-start | bytes 786440 | tf_op jit(solution)/shard_map/ppermute | solution.py:23
  10.9 8.3 %collective-permute-start = (bf16[128,1024]{1,0:T(8,128)(2,1)}, bf16[128,1024]{1,0:T(8,128)(2,1)S(1)}, u32[]{:S(2)}, u32[]{:S(2)}) collective-permute-start(bf16[128,1024]{1,0:T(8,128)(2,1)} %param.6), channel_id=1, source_target_pairs={{0,1},{1,2},{2,3},{3,0},{4,5},{5,6},{6,7},{7,4},{8,9},{9,10},{10,1... | collective-permute-start | bytes 786440 | tf_op jit(solution)/shard_map/ppermute | solution.py:18
  19.2 7.3 %collective-permute-start.2 = (bf16[128,1024]{1,0:T(8,128)(2,1)S(1)}, bf16[128,1024]{1,0:T(8,128)(2,1)S(1)}, u32[]{:S(2)}, u32[]{:S(2)}) collective-permute-start(bf16[128,1024]{1,0:T(8,128)(2,1)S(1)} %collective-permute-done), channel_id=1, source_target_pairs={{0,1},{1,2},{2,3},{3,0},{4,5},{5,6},{6,7},{7,4},{8,9},{9,10},{10,1... | collective-permute-start | bytes 786440 | tf_op jit(solution)/shard_map/ppermute | solution.py:18
  20.0 28.1 %copy-start = (bf16[128,8,128]{2,0,1:T(8,128)(2,1)}, bf16[128,8,128]{2,0,1:T(8,128)(2,1)S(1)}, u32[]{:S(2)}) copy-start(bf16[128,8,128]{2,0,1:T(8,128)(2,1)S(1)} %copy.41) | copy-start | bytes 786436
Sparse Core Ops, SparseCore 0:
  52.5 144.3 all-gather.2
